TPU v7x, 256 devices: a whole 4x4x8 slice. The times are simulated.
256 devices in a mesh: ctx: 256 (over z, y, x, core).
Axes of the slice: x: 4, y: 4, z: 8, core: 2. Of those that a mesh axis runs over, the one named last changes fastest.
Arguments:
- queries: bfloat16 [131072, 1024], P('ctx'), may hold values from -6 to 6
- key_rows: bfloat16 [131072, 128], P('ctx'), may hold values from -6 to 6
- value_rows: bfloat16 [131072, 128], P('ctx'), may hold values from -6 to 6
- grad_out: bfloat16 [131072, 1024], P('ctx'), may hold values from -16 to 16
- attn_out: bfloat16 [131072, 1024], P('ctx'), may hold values from -6 to 6
- log_total: float32 [8, 131072], P(None, 'ctx'), as said below
- block_pair: int32 [256], P('ctx'), may hold values from 0 to 255, as said below
Outputs:
- grad_queries: bfloat16 [131072, 1024], P('ctx')
- grad_keys: bfloat16 [131072, 128], P('ctx')
- grad_values: bfloat16 [131072, 128], P('ctx')
Inputs may be any that keep to these rules, and one draw needn't show every extreme that they name: `log_total`: the log of the sum of exp(scores) over the visible keys of each head and row. `block_pair`: each block number appears once.
All inputs are finite; a program needn't handle non-finite values.
Results may differ from a plain program's by a relative error of at most 0.0073.
Values may be sent and summed in bfloat16 or wider, within the bound.
No kernel may reach another device: no remote copies, remote signals or barrier semaphores. Data moves between devices by JAX's collectives and lax.ppermute only.
A program may use at most 64 MiB of HBM per device.

v0:
```python
import functools

import jax
import jax.numpy as jnp
from jax import lax
from jax.experimental import pallas as pl
from jax.experimental.pallas import tpu as pltpu
from jax.sharding import PartitionSpec as P

STEPS = 4


def passed_along(value, axis, steps):
    count = lax.axis_size(axis)
    pairs = [(source, (source + steps) % count) for source in range(count)]
    return lax.ppermute(value, axis, pairs)


def tile_body(tiles, has_in, half, width, scale,
              info_ref, q_ref, do_ref, kv_ref, lse_ref, dl_ref, *rest):
    if has_in:
        dqin_ref, dq_ref, dkv_ref, acc_ref = rest
    else:
        dq_ref, dkv_ref, acc_ref = rest
    head = pl.program_id(0)

    @pl.when(head == 0)
    def _():
        dkv_ref[...] = jnp.zeros_like(dkv_ref)

    if has_in:
        acc_ref[...] = dqin_ref[...]
    else:
        acc_ref[...] = jnp.zeros_like(acc_ref)
    other = info_ref[0]
    for q_sel, k_sel, diag in tiles:
        qi = other if q_sel is None else q_sel
        ki = other if k_sel is None else k_sel
        q_rows = pl.ds(pl.multiple_of(qi * half, half), half)
        k_rows = pl.ds(pl.multiple_of(ki * half, half), half)
        q = q_ref[q_rows, :]
        do = do_ref[q_rows, :]
        k = kv_ref[k_rows, pl.ds(0, width)]
        v = kv_ref[k_rows, pl.ds(width, width)]
        lse = lse_ref[0, qi]
        dl = dl_ref[0, qi]
        s_t = lax.dot_general(k, q, (((1,), (1,)), ((), ())),
                              preferred_element_type=jnp.float32) * scale
        p_t = jnp.exp(s_t - lse)
        if diag:
            rows = lax.broadcasted_iota(jnp.int32, (half, half), 0)
            cols = lax.broadcasted_iota(jnp.int32, (half, half), 1)
            p_t = jnp.where(rows <= cols, p_t, 0.0)
        dp_t = lax.dot_general(v, do, (((1,), (1,)), ((), ())),
                               preferred_element_type=jnp.float32)
        ds_t = (p_t * (dp_t - dl) * scale).astype(jnp.bfloat16)
        pb_t = p_t.astype(jnp.bfloat16)
        dv = jnp.dot(pb_t, do, preferred_element_type=jnp.float32)
        dk = jnp.dot(ds_t, q, preferred_element_type=jnp.float32)
        dq = lax.dot_general(ds_t, k, (((0,), (0,)), ((), ())),
                             preferred_element_type=jnp.float32)
        acc_ref[q_rows, :] += dq
        dkv_ref[k_rows, pl.ds(0, width)] += dk
        dkv_ref[k_rows, pl.ds(width, width)] += dv
    dq_ref[...] = acc_ref[...].astype(dq_ref.dtype)


def tile_step(tiles, info, queries, grad_out, kv, lse4, delta4, dq_in, dq_dtype):
    rows, cols = queries.shape
    width = kv.shape[1] // 2
    heads = cols // width
    half = rows // 2
    scale = width ** (-0.5)
    has_in = dq_in is not None
    col_spec = pl.BlockSpec((rows, width), lambda h, info: (0, h))
    kv_spec = pl.BlockSpec((rows, 2 * width), lambda h, info: (0, 0))
    row_spec = pl.BlockSpec((1, 2, 1, half), lambda h, info: (h, 0, 0, 0))
    in_specs = [col_spec, col_spec, kv_spec, row_spec, row_spec]
    args = [queries, grad_out, kv, lse4, delta4]
    aliases = {}
    if has_in:
        in_specs.append(col_spec)
        args.append(dq_in)
        if dq_in.dtype == dq_dtype:
            aliases = {len(args): 0}
    flops = len(tiles) * heads * 5 * 2 * half * half * width
    nbytes = 2 * rows * cols * 2 + rows * 2 * width * 2 + rows * cols * 4 * (2 if has_in else 1)
    return pl.pallas_call(
        functools.partial(tile_body, tiles, has_in, half, width, scale),
        out_shape=(
            jax.ShapeDtypeStruct((rows, cols), dq_dtype),
            jax.ShapeDtypeStruct((rows, 2 * width), jnp.float32),
        ),
        grid_spec=pltpu.PrefetchScalarGridSpec(
            num_scalar_prefetch=1,
            grid=(heads,),
            in_specs=in_specs,
            out_specs=[col_spec, kv_spec],
            scratch_shapes=[pltpu.VMEM((rows, width), jnp.float32)],
        ),
        input_output_aliases=aliases,
        compiler_params=pltpu.CompilerParams(dimension_semantics=("arbitrary",)),
        cost_estimate=pl.CostEstimate(
            flops=flops, transcendentals=len(tiles) * heads * half * half, bytes_accessed=nbytes
        ),
    )(info, *args)


OWN_TILES = ((0, 0, True), (1, 0, False), (1, 1, True))
VISIT_TILES = ((1, 0, False), (None, None, False))


def on_device(queries, key_rows, value_rows, grad_out, attn_out, log_total, block_pair):
    rows, width = key_rows.shape
    half = rows // 2
    heads = queries.shape[1] // width
    own_block = block_pair[0]
    kv = jnp.concatenate([key_rows, value_rows], axis=1)
    delta = jnp.einsum(
        "qhd,qhd->hq",
        grad_out.reshape(rows, heads, width),
        attn_out.reshape(rows, heads, width),
        preferred_element_type=jnp.float32,
    )
    lse4 = log_total.reshape(heads, 2, 1, half)
    delta4 = delta.reshape(heads, 2, 1, half)

    visitors = [(kv, block_pair)]
    moving = (kv, block_pair)
    for _ in range(1, STEPS):
        moving = passed_along(moving, "ctx", 1)
        visitors.append(moving)

    zero_info = jnp.zeros((1,), jnp.int32)
    dq, sums = tile_step(OWN_TILES, zero_info, queries, grad_out, kv, lse4, delta4,
                         None, jnp.float32)
    for step in range(1, STEPS):
        received = passed_along(sums, "ctx", 1)
        kv_s, block_s = visitors[step]
        other = jnp.where(block_s[0] < own_block, 0, 1).astype(jnp.int32).reshape(1)
        last = step == STEPS - 1
        dq, part = tile_step(VISIT_TILES, other, queries, grad_out, kv_s, lse4, delta4,
                             dq, jnp.bfloat16 if last else jnp.float32)
        sums = received + part
    final = passed_along(sums.astype(jnp.bfloat16), "ctx", 1 - STEPS)
    return dq, final[:, :width], final[:, width:]


def solution(mesh):
    return jax.shard_map(
        on_device,
        mesh=mesh,
        in_specs=(
            P("ctx", None),
            P("ctx", None),
            P("ctx", None),
            P("ctx", None),
            P("ctx", None),
            P(None, "ctx"),
            P("ctx"),
        ),
        out_specs=(P("ctx", None), P("ctx", None), P("ctx", None)),
        check_vma=False,
    )
```

profile of v0, /device:TPU:125, one launch (start us, length us, event | category | flops | bytes accessed | tf_op | source)
XLA Modules:
  0.0 112.4 jit_solution(8621733845535907476)
XLA Ops:
  0.6 0.0 copy-start
  0.6 1.6 %copy.21 = bf16[64,8,8,128]{3,2,1,0:T(8,128)(2,1)S(1)} copy(bf16[64,8,8,128]{3,1,2,0:T(8,128)(2,1)} %bitcast.13) | data formatting | bytes 2097152
  2.2 0.0 copy-done
  2.2 0.0 copy-start.4
  2.2 0.0 copy-start.1
  2.3 0.0 copy-start.2
  2.3 0.3 copy.22
  2.5 0.6 fusion
  3.2 0.7 copy.20.dl_ref
  3.9 0.0 copy-done.4
  3.9 0.6 reshape.36.lse_ref
  4.5 0.0 copy-done.1
  4.6 0.0 copy-done.2
  4.6 0.0 copy-start.3
  4.6 0.7 copy-done.3
  5.3 11.4 %shard_map.94 = (f32[512,1024]{1,0:T(8,128)}, f32[512,256]{1,0:T(8,128)}) custom-call(s32[1]{0:T(128)} %constant.9.clone.1.info_ref, bf16[512,1024]{1,0:T(8,128)(2,1)} %q_ref.7, bf16[512,1024]{1,0:T(8,128)(2,1)} %do_ref.7, bf16[512,256]{1,0:T(8,128)(2,1)} %copy-done.3, f32[8,2,1,256]{3,2,1,0:T(1,128)} %reshape.36.lse_ref, f32[8,2,1,256]{3,2,1,0:T(1,128)} %copy.20.dl_ref), custom_call_target="tpu_custom_call" | custom-call | flops 2013265920 | bytes 4456448 | tf_op jit(solution)/shard_map/pallas_call | solution.py:88
  16.7 1.5 %collective-permute-start.6 = (f32[512,256]{1,0:T(8,128)}, f32[512,256]{1,0:T(8,128)S(1)}, u32[]{:S(2)}, u32[]{:S(2)}) collective-permute-start(f32[512,256]{1,0:T(8,128)} %get-tuple-element.15), channel_id=1, source_target_pairs={{0,1},{1,2},{2,3},{3,4},{4,5},{5,6},{6,7},{7,8},{8,9},{9,10},{10,1... | collective-permute-start | bytes 1572872 | tf_op jit(solution)/shard_map/ppermute | solution.py:16
  18.2 0.1 collective-permute-start.3
  18.2 2.7 %collective-permute-start = (s32[1]{0:T(128)}, s32[1]{0:T(128)}, u32[]{:S(2)}, u32[]{:S(2)}) collective-permute-start(s32[1]{0:T(128)} %param.13), channel_id=1, source_target_pairs={{0,1},{1,2},{2,3},{3,4},{4,5},{5,6},{6,7},{7,8},{8,9},{9,10},{10,1... | collective-permute-start | bytes 20 | tf_op jit(solution)/shard_map/ppermute | solution.py:16
  21.7 5.8 %collective-permute-done = s32[1]{0:T(128)} collective-permute-done((s32[1]{0:T(128)}, s32[1]{0:T(128)}, u32[]{:S(2)}, u32[]{:S(2)}) %collective-permute-start) | collective-permute-done | bytes 36 | tf_op jit(solution)/shard_map/ppermute | solution.py:16
  28.1 0.0 collective-permute-done.3.kv_ref
  28.1 0.0 copy-start.6
  28.1 0.7 copy-done.6
  28.8 9.9 %shard_map.95 = (f32[512,1024]{1,0:T(8,128)}, f32[512,256]{1,0:T(8,128)}) custom-call(s32[1]{0:T(128)S(6)} %select_n.15.info_ref, bf16[512,1024]{1,0:T(8,128)(2,1)} %q_ref.7, bf16[512,1024]{1,0:T(8,128)(2,1)} %do_ref.7, bf16[512,256]{1,0:T(8,128)(2,1)} %copy-done.6, f32[8,2,1,256]{3,2,1,0:T(1,128)} %reshape.36.lse_ref, ...), custom_call_target="tpu_custom_call", output_to_operand_aliasing={{0}: (6, {})} | custom-call | flops 1342177280 | bytes 6553600 | tf_op jit(solution)/shard_map/pallas_call | solution.py:88
  38.7 0.0 collective-permute-done.6
  38.7 1.1 add.9
  39.8 2.5 %collective-permute-start.7 = (f32[512,256]{1,0:T(8,128)S(1)}, f32[512,256]{1,0:T(8,128)S(1)}, u32[]{:S(2)}, u32[]{:S(2)}) collective-permute-start(f32[512,256]{1,0:T(8,128)S(1)} %add.9), channel_id=1, source_target_pairs={{0,1},{1,2},{2,3},{3,4},{4,5},{5,6},{6,7},{7,8},{8,9},{9,10},{10,1... | collective-permute-start | bytes 1572872 | tf_op jit(solution)/shard_map/ppermute | solution.py:16
  42.3 0.4 collective-permute-start.4
  42.7 7.8 %collective-permute-start.1 = (s32[1]{0:T(128)}, s32[1]{0:T(128)}, u32[]{:S(2)}, u32[]{:S(2)}) collective-permute-start(s32[1]{0:T(128)} %collective-permute-done), channel_id=1, source_target_pairs={{0,1},{1,2},{2,3},{3,4},{4,5},{5,6},{6,7},{7,8},{8,9},{9,10},{10,1... | collective-permute-start | bytes 20 | tf_op jit(solution)/shard_map/ppermute | solution.py:16
  50.5 0.9 collective-permute-done.1
  52.1 0.0 collective-permute-done.4.kv_ref
  52.2 0.0 copy-start.5
  52.2 0.7 copy-done.5
  52.9 9.9 %shard_map.96 = (f32[512,1024]{1,0:T(8,128)}, f32[512,256]{1,0:T(8,128)}) custom-call(s32[1]{0:T(128)S(6)} %select_n.14.info_ref, bf16[512,1024]{1,0:T(8,128)(2,1)} %q_ref.7, bf16[512,1024]{1,0:T(8,128)(2,1)} %do_ref.7, bf16[512,256]{1,0:T(8,128)(2,1)} %copy-done.5, f32[8,2,1,256]{3,2,1,0:T(1,128)} %reshape.36.lse_ref, ...), custom_call_target="tpu_custom_call", output_to_operand_aliasing={{0}: (6, {})} | custom-call | flops 1342177280 | bytes 6553600 | tf_op jit(solution)/shard_map/pallas_call | solution.py:88
  62.7 0.0 collective-permute-done.7
  62.7 1.1 add.10
  63.8 2.4 %collective-permute-start.8 = (f32[512,256]{1,0:T(8,128)S(1)}, f32[512,256]{1,0:T(8,128)S(1)}, u32[]{:S(2)}, u32[]{:S(2)}) collective-permute-start(f32[512,256]{1,0:T(8,128)S(1)} %add.10), channel_id=1, source_target_pairs={{0,1},{1,2},{2,3},{3,4},{4,5},{5,6},{6,7},{7,8},{8,9},{9,10},{10,1... | collective-permute-start | bytes 1572872 | tf_op jit(solution)/shard_map/ppermute | solution.py:16
  66.2 5.8 %collective-permute-start.5 = (bf16[512,256]{1,0:T(8,128)(2,1)}, bf16[512,256]{1,0:T(8,128)(2,1)S(1)}, u32[]{:S(2)}, u32[]{:S(2)}) collective-permute-start(bf16[512,256]{1,0:T(8,128)(2,1)} %copy-done.5), channel_id=1, source_target_pairs={{0,1},{1,2},{2,3},{3,4},{4,5},{5,6},{6,7},{7,8},{8,9},{9,10},{10,1... | collective-permute-start | bytes 786440 | tf_op jit(solution)/shard_map/ppermute | solution.py:16
  72.0 7.9 %collective-permute-start.2 = (s32[1]{0:T(128)}, s32[1]{0:T(128)}, u32[]{:S(2)}, u32[]{:S(2)}) collective-permute-start(s32[1]{0:T(128)} %collective-permute-done.1), channel_id=1, source_target_pairs={{0,1},{1,2},{2,3},{3,4},{4,5},{5,6},{6,7},{7,8},{8,9},{9,10},{10,1... | collective-permute-start | bytes 20 | tf_op jit(solution)/shard_map/ppermute | solution.py:16
  79.9 0.9 collective-permute-done.2
  81.4 0.0 collective-permute-done.5.kv_ref
  81.5 0.7 copy-done.7
  82.2 9.6 %shard_map.97 = (bf16[512,1024]{1,0:T(8,128)(2,1)}, f32[512,256]{1,0:T(8,128)}) custom-call(s32[1]{0:T(128)S(6)} %select_n.13.info_ref, bf16[512,1024]{1,0:T(8,128)(2,1)} %q_ref.7, bf16[512,1024]{1,0:T(8,128)(2,1)} %do_ref.7, bf16[512,256]{1,0:T(8,128)(2,1)} %copy-done.7, f32[8,2,1,256]{3,2,1,0:T(1,128)} %reshape.36.lse_ref, f32[8,2,1,256]{3,2,1,0:T(1,128)} %copy.20.dl_ref, ...), custom_call_target="tpu_custom_call" | custom-call | flops 1342177280 | bytes 6553600 | tf_op jit(solution)/shard_map/pallas_call | solution.py:88
  91.8 0.0 collective-permute-done.8
  91.8 1.1 add_convert_fusion
  92.9 0.1 collective-permute-start.9
  93.0 18.7 %collective-permute-done.9 = bf16[512,256]{1,0:T(8,128)(2,1)S(1)} collective-permute-done((bf16[512,256]{1,0:T(8,128)(2,1)S(1)}, bf16[512,256]{1,0:T(8,128)(2,1)S(1)}, u32[]{:S(2)}, u32[]{:S(2)}) %collective-permute-start.9) | collective-permute-done | bytes 262176 | tf_op jit(solution)/shard_map/ppermute | solution.py:16
  111.7 0.7 fusion.1
  (3 shorter events, 0.1 us)
Async XLA Ops:
  0.6 1.6 %copy-start = (bf16[512,1024]{1,0:T(8,128)(2,1)S(1)}, bf16[512,1024]{1,0:T(8,128)(2,1)}, u32[]{:S(2)}) copy-start(bf16[512,1024]{1,0:T(8,128)(2,1)} %param.11) | copy-start | bytes 3145732
  2.2 1.7 %copy-start.4 = (f32[8,512]{1,0:T(8,128)S(1)}, f32[8,512]{1,0:T(8,128)}, u32[]{:S(2)}) copy-start(f32[8,512]{1,0:T(8,128)} %param.12) | copy-start | bytes 49156
  2.2 2.3 %copy-start.1 = (bf16[512,128]{1,0:T(8,128)(2,1)S(1)}, bf16[512,128]{1,0:T(8,128)(2,1)}, u32[]{:S(2)}) copy-start(bf16[512,128]{1,0:T(8,128)(2,1)} %param.8) | copy-start | bytes 393220
  2.3 2.3 %copy-start.2 = (bf16[512,128]{1,0:T(8,128)(2,1)S(1)}, bf16[512,128]{1,0:T(8,128)(2,1)}, u32[]{:S(2)}) copy-start(bf16[512,128]{1,0:T(8,128)(2,1)} %param.9) | copy-start | bytes 393220
  4.6 0.7 copy-start.3
  16.7 22.0 %collective-permute-start.6 = (f32[512,256]{1,0:T(8,128)}, f32[512,256]{1,0:T(8,128)S(1)}, u32[]{:S(2)}, u32[]{:S(2)}) collective-permute-start(f32[512,256]{1,0:T(8,128)} %get-tuple-element.15), channel_id=1, source_target_pairs={{0,1},{1,2},{2,3},{3,4},{4,5},{5,6},{6,7},{7,8},{8,9},{9,10},{10,1... | collective-permute-start | bytes 1572872 | tf_op jit(solution)/shard_map/ppermute | solution.py:16
  18.2 9.9 %collective-permute-start.3 = (bf16[512,256]{1,0:T(8,128)(2,1)}, bf16[512,256]{1,0:T(8,128)(2,1)S(1)}, u32[]{:S(2)}, u32[]{:S(2)}) collective-permute-start(bf16[512,256]{1,0:T(8,128)(2,1)} %copy-done.3), channel_id=1, source_target_pairs={{0,1},{1,2},{2,3},{3,4},{4,5},{5,6},{6,7},{7,8},{8,9},{9,10},{10,1... | collective-permute-start | bytes 786440 | tf_op jit(solution)/shard_map/ppermute | solution.py:16
  18.2 9.2 %collective-permute-start = (s32[1]{0:T(128)}, s32[1]{0:T(128)}, u32[]{:S(2)}, u32[]{:S(2)}) collective-permute-start(s32[1]{0:T(128)} %param.13), channel_id=1, source_target_pairs={{0,1},{1,2},{2,3},{3,4},{4,5},{5,6},{6,7},{7,8},{8,9},{9,10},{10,1... | collective-permute-start | bytes 20 | tf_op jit(solution)/shard_map/ppermute | solution.py:16
  28.1 0.7 copy-start.6
  39.8 22.9 %collective-permute-start.7 = (f32[512,256]{1,0:T(8,128)S(1)}, f32[512,256]{1,0:T(8,128)S(1)}, u32[]{:S(2)}, u32[]{:S(2)}) collective-permute-start(f32[512,256]{1,0:T(8,128)S(1)} %add.9), channel_id=1, source_target_pairs={{0,1},{1,2},{2,3},{3,4},{4,5},{5,6},{6,7},{7,8},{8,9},{9,10},{10,1... | collective-permute-start | bytes 1572872 | tf_op jit(solution)/shard_map/ppermute | solution.py:16
  42.3 9.9 %collective-permute-start.4 = (bf16[512,256]{1,0:T(8,128)(2,1)}, bf16[512,256]{1,0:T(8,128)(2,1)S(1)}, u32[]{:S(2)}, u32[]{:S(2)}) collective-permute-start(bf16[512,256]{1,0:T(8,128)(2,1)} %copy-done.6), channel_id=1, source_target_pairs={{0,1},{1,2},{2,3},{3,4},{4,5},{5,6},{6,7},{7,8},{8,9},{9,10},{10,1... | collective-permute-start | bytes 786440 | tf_op jit(solution)/shard_map/ppermute | solution.py:16
  42.7 8.8 %collective-permute-start.1 = (s32[1]{0:T(128)}, s32[1]{0:T(128)}, u32[]{:S(2)}, u32[]{:S(2)}) collective-permute-start(s32[1]{0:T(128)} %collective-permute-done), channel_id=1, source_target_pairs={{0,1},{1,2},{2,3},{3,4},{4,5},{5,6},{6,7},{7,8},{8,9},{9,10},{10,1... | collective-permute-start | bytes 20 | tf_op jit(solution)/shard_map/ppermute | solution.py:16
  52.2 0.7 copy-start.5
  63.8 28.0 %collective-permute-start.8 = (f32[512,256]{1,0:T(8,128)S(1)}, f32[512,256]{1,0:T(8,128)S(1)}, u32[]{:S(2)}, u32[]{:S(2)}) collective-permute-start(f32[512,256]{1,0:T(8,128)S(1)} %add.10), channel_id=1, source_target_pairs={{0,1},{1,2},{2,3},{3,4},{4,5},{5,6},{6,7},{7,8},{8,9},{9,10},{10,1... | collective-permute-start | bytes 1572872 | tf_op jit(solution)/shard_map/ppermute | solution.py:16
  66.2 15.2 %collective-permute-start.5 = (bf16[512,256]{1,0:T(8,128)(2,1)}, bf16[512,256]{1,0:T(8,128)(2,1)S(1)}, u32[]{:S(2)}, u32[]{:S(2)}) collective-permute-start(bf16[512,256]{1,0:T(8,128)(2,1)} %copy-done.5), channel_id=1, source_target_pairs={{0,1},{1,2},{2,3},{3,4},{4,5},{5,6},{6,7},{7,8},{8,9},{9,10},{10,1... | collective-permute-start | bytes 786440 | tf_op jit(solution)/shard_map/ppermute | solution.py:16
  72.0 8.8 %collective-permute-start.2 = (s32[1]{0:T(128)}, s32[1]{0:T(128)}, u32[]{:S(2)}, u32[]{:S(2)}) collective-permute-start(s32[1]{0:T(128)} %collective-permute-done.1), channel_id=1, source_target_pairs={{0,1},{1,2},{2,3},{3,4},{4,5},{5,6},{6,7},{7,8},{8,9},{9,10},{10,1... | collective-permute-start | bytes 20 | tf_op jit(solution)/shard_map/ppermute | solution.py:16
  81.5 0.7 copy-start.7
  92.9 18.8 %collective-permute-start.9 = (bf16[512,256]{1,0:T(8,128)(2,1)S(1)}, bf16[512,256]{1,0:T(8,128)(2,1)S(1)}, u32[]{:S(2)}, u32[]{:S(2)}) collective-permute-start(bf16[512,256]{1,0:T(8,128)(2,1)S(1)} %add_convert_fusion), channel_id=1, source_target_pairs={{0,253},{1,254},{2,255},{3,0},{4,1},{5,2},{6,3},{7,4},{8,5},{9,6},... | collective-permute-start | bytes 786440 | tf_op jit(solution)/shard_map/ppermute | solution.py:16
where the time goes:
time: 113 us; the launch traced here: 112 us
  Pallas kernels  40.7 us (36%)
  starting transfers between devices  31.1 us (28%)
  waiting for transfers between devices  26.3 us (23%)
  local copies, waits for them, and re-layouts  6.79 us (6%)
  other arithmetic  3.95 us (3%)
  between operations  3.5 us (3%)
    pallas_call x4, Pallas kernels, tile_step(): pl.pallas_call(functools.partial(tile_body, tiles, has_in, half, width, s...  40.7 us
    ppermute x10, starting transfers between devices, passed_along(): return lax.ppermute(value, axis, pairs)  31.1 us
    ppermute x10, waiting for transfers between devices, passed_along(): return lax.ppermute(value, axis, pairs)  26.3 us
    unnamed x19, local copies, waits for them, and re-layouts  4.7 us
  transfers between devices with their start and end apart: 10, of which 4 were waited for; matrix products, arithmetic and copies ran while one was open for 0% of the time, Pallas kernels for 26%

commit v1 on v0

v1 whole, which is shorter than its diff:
```python
import functools

import jax
import jax.numpy as jnp
from jax import lax
from jax.experimental import pallas as pl
from jax.experimental.pallas import tpu as pltpu
from jax.sharding import PartitionSpec as P


STEPS = 4


def passed_along(value, axis, steps):
    count = lax.axis_size(axis)
    pairs = [(source, (source + steps) % count) for source in range(count)]
    return lax.ppermute(value, axis, pairs)


def tile_body(tiles, has_in, group, half, width, scale,
              info_ref, q_ref, do_ref, kv_ref, lse_ref, dl_ref, *rest):
    if has_in:
        dqin_ref, dq_ref, dkv_ref, acc_ref = rest
    else:
        dq_ref, dkv_ref, acc_ref = rest
    block = pl.program_id(0)

    @pl.when(block == 0)
    def _():
        dkv_ref[...] = jnp.zeros_like(dkv_ref)

    if has_in:
        acc_ref[...] = dqin_ref[...]
    else:
        acc_ref[...] = jnp.zeros_like(acc_ref)
    other = info_ref[0]
    for j in range(group):
        head = block * group + j
        cols = pl.ds(j * width, width)
        lse_all = lse_ref[pl.ds(head, 1), :]
        dl_all = dl_ref[pl.ds(head, 1), :]
        for q_sel, k_sel, diag in tiles:
            if q_sel is None:
                qi = other
                lse = jnp.where(other == 0, lse_all[:, :half], lse_all[:, half:])
                dl = jnp.where(other == 0, dl_all[:, :half], dl_all[:, half:])
            else:
                qi = q_sel
                lse = lse_all[:, q_sel * half:(q_sel + 1) * half]
                dl = dl_all[:, q_sel * half:(q_sel + 1) * half]
            ki = other if k_sel is None else k_sel
            q_rows = pl.ds(pl.multiple_of(qi * half, half), half)
            k_rows = pl.ds(pl.multiple_of(ki * half, half), half)
            q = q_ref[q_rows, cols]
            do = do_ref[q_rows, cols]
            k = kv_ref[k_rows, pl.ds(0, width)]
            v = kv_ref[k_rows, pl.ds(width, width)]
            s_t = lax.dot_general(k, q, (((1,), (1,)), ((), ())),
                                  preferred_element_type=jnp.float32) * scale
            p_t = jnp.exp(s_t - lse)
            if diag:
                rows = lax.broadcasted_iota(jnp.int32, (half, half), 0)
                cols_i = lax.broadcasted_iota(jnp.int32, (half, half), 1)
                p_t = jnp.where(rows <= cols_i, p_t, 0.0)
            dp_t = lax.dot_general(v, do, (((1,), (1,)), ((), ())),
                                   preferred_element_type=jnp.float32)
            ds_t = (p_t * (dp_t - dl) * scale).astype(jnp.bfloat16)
            pb_t = p_t.astype(jnp.bfloat16)
            dv = jnp.dot(pb_t, do, preferred_element_type=jnp.float32)
            dk = jnp.dot(ds_t, q, preferred_element_type=jnp.float32)
            dq = lax.dot_general(ds_t, k, (((0,), (0,)), ((), ())),
                                 preferred_element_type=jnp.float32)
            acc_ref[q_rows, cols] += dq
            dkv_ref[k_rows, pl.ds(0, width)] += dk
            dkv_ref[k_rows, pl.ds(width, width)] += dv
    dq_ref[...] = acc_ref[...].astype(dq_ref.dtype)


GROUP = 4


def tile_step(tiles, info, queries, grad_out, kv, lse, delta, dq_in, dq_dtype):
    rows, cols = queries.shape
    width = kv.shape[1] // 2
    heads = cols // width
    half = rows // 2
    scale = width ** (-0.5)
    has_in = dq_in is not None
    col_spec = pl.BlockSpec((rows, GROUP * width), lambda g, info: (0, g))
    kv_spec = pl.BlockSpec((rows, 2 * width), lambda g, info: (0, 0))
    row_spec = pl.BlockSpec((heads, rows), lambda g, info: (0, 0))
    in_specs = [col_spec, col_spec, kv_spec, row_spec, row_spec]
    args = [queries, grad_out, kv, lse, delta]
    aliases = {}
    if has_in:
        in_specs.append(col_spec)
        args.append(dq_in)
        if dq_in.dtype == dq_dtype:
            aliases = {len(args): 0}
    flops = len(tiles) * heads * 5 * 2 * half * half * width
    nbytes = 2 * rows * cols * 2 + rows * 2 * width * 2 + rows * cols * 4 * (2 if has_in else 1)
    return pl.pallas_call(
        functools.partial(tile_body, tiles, has_in, GROUP, half, width, scale),
        out_shape=(
            jax.ShapeDtypeStruct((rows, cols), dq_dtype),
            jax.ShapeDtypeStruct((rows, 2 * width), jnp.float32),
        ),
        grid_spec=pltpu.PrefetchScalarGridSpec(
            num_scalar_prefetch=1,
            grid=(heads // GROUP,),
            in_specs=in_specs,
            out_specs=[col_spec, kv_spec],
            scratch_shapes=[pltpu.VMEM((rows, GROUP * width), jnp.float32)],
        ),
        input_output_aliases=aliases,
        compiler_params=pltpu.CompilerParams(dimension_semantics=("arbitrary",)),
        cost_estimate=pl.CostEstimate(
            flops=flops, transcendentals=len(tiles) * heads * half * half, bytes_accessed=nbytes
        ),
    )(info, *args)


OWN_TILES = ((0, 0, True), (1, 0, False), (1, 1, True))
VISIT_TILES = ((1, 0, False), (None, None, False))


def device_steps(queries, key_rows, value_rows, grad_out, attn_out, log_total, block_pair):
    rows, width = key_rows.shape
    heads = queries.shape[1] // width
    own_block = block_pair[0]
    kv = jnp.concatenate([key_rows, value_rows], axis=1)
    delta = jnp.einsum(
        "qhd,qhd->hq",
        grad_out.reshape(rows, heads, width),
        attn_out.reshape(rows, heads, width),
        preferred_element_type=jnp.float32,
    )

    visitors = [(kv, block_pair)]
    for step in range(1, STEPS):
        visitors.append(passed_along((kv, block_pair), "ctx", step))

    zero_info = jnp.zeros((1,), jnp.int32)
    dq, sums = tile_step(OWN_TILES, zero_info, queries, grad_out, kv, log_total, delta,
                         None, jnp.float32)
    for step in range(1, STEPS):
        received = passed_along(sums, "ctx", 1)
        kv_s, block_s = visitors[step]
        other = jnp.where(block_s[0] < own_block, 0, 1).astype(jnp.int32).reshape(1)
        last = step == STEPS - 1
        dq, part = tile_step(VISIT_TILES, other, queries, grad_out, kv_s, log_total, delta,
                             dq, jnp.bfloat16 if last else jnp.float32)
        sums = received + part
    final = passed_along(sums.astype(jnp.bfloat16), "ctx", 1 - STEPS)
    return dq, final[:, :width], final[:, width:]


def solution(mesh):
    return jax.shard_map(
        device_steps,
        mesh=mesh,
        in_specs=(
            P("ctx", None),
            P("ctx", None),
            P("ctx", None),
            P("ctx", None),
            P("ctx", None),
            P(None, "ctx"),
            P("ctx"),
        ),
        out_specs=(P("ctx", None), P("ctx", None), P("ctx", None)),
        check_vma=False,
    )
```

time: 113 us -> 111 us (0.982)
  the two profiles are of different devices: /device:TPU:125 before, /device:TPU:1 now
where the time goes in v1:
time: 111 us
  waiting for transfers between devices  52.9 us (48%)
  Pallas kernels  34.2 us (31%)
  starting transfers between devices  9.14 us (8%)
  local copies, waits for them, and re-layouts  7.06 us (6%)
  other arithmetic  3.95 us (4%)
  between operations  3.53 us (3%)
    ppermute x10, waiting for transfers between devices, passed_along(): return lax.ppermute(value, axis, pairs)  52.9 us
    pallas_call x4, Pallas kernels, tile_step(): pl.pallas_call(functools.partial(tile_body, tiles, has_in, GROUP, half, w...  34.2 us
    ppermute x10, starting transfers between devices, passed_along(): return lax.ppermute(value, axis, pairs)  9.14 us
    unnamed x17, local copies, waits for them, and re-layouts  5.6 us
  transfers between devices with their start and end apart: 10, of which 4 were waited for; matrix products, arithmetic and copies ran while one was open for 0% of the time, Pallas kernels for 22%

profile of v1, /device:TPU:1, one launch (start us, length us, event | category | flops | bytes accessed | tf_op | source)
XLA Modules:
  0.0 110.7 jit_solution(7347130242532979915)
XLA Ops:
  0.6 0.0 copy-start
  0.6 1.0 constant_dynamic-update-slice_fusion.1
  1.7 1.5 %copy.21 = bf16[64,8,8,128]{3,2,1,0:T(8,128)(2,1)S(1)} copy(bf16[64,8,8,128]{3,1,2,0:T(8,128)(2,1)} %bitcast.10) | data formatting | bytes 2097152
  3.2 0.0 copy-done
  3.2 0.0 copy-start.1
  3.2 0.3 copy.20
  3.5 0.6 fusion
  4.1 0.7 copy.18.dl_ref
  4.8 0.0 copy-done.1
  4.9 0.0 copy-start.2
  4.9 0.7 copy-done.2
  5.6 10.0 %shard_map.94 = (f32[512,1024]{1,0:T(8,128)}, f32[512,256]{1,0:T(8,128)}) custom-call(s32[1]{0:T(128)} %constant.9.clone.1.info_ref, bf16[512,1024]{1,0:T(8,128)(2,1)} %q_ref.7, bf16[512,1024]{1,0:T(8,128)(2,1)} %do_ref.7, bf16[512,256]{1,0:T(8,128)(2,1)} %copy-done.2, f32[8,512]{1,0:T(8,128)} %lse_ref.7, f32[8,512]{1,0:T(8,128)} %copy.18.dl_ref), custom_call_target="tpu_custom_call" | custom-call | flops 2013265920 | bytes 4456448 | tf_op jit(solution)/shard_map/pallas_call | solution.py:102
  15.5 2.6 %collective-permute-start.6 = (f32[512,256]{1,0:T(8,128)}, f32[512,256]{1,0:T(8,128)S(1)}, u32[]{:S(2)}, u32[]{:S(2)}) collective-permute-start(f32[512,256]{1,0:T(8,128)} %get-tuple-element.15), channel_id=1, source_target_pairs={{0,1},{1,2},{2,3},{3,4},{4,5},{5,6},{6,7},{7,8},{8,9},{9,10},{10,1... | collective-permute-start | bytes 1572872 | tf_op jit(solution)/shard_map/ppermute | solution.py:17
  18.1 0.0 collective-permute-start.5
  18.2 1.6 %collective-permute-start.4 = (s32[1]{0:T(128)}, s32[1]{0:T(128)}, u32[]{:S(2)}, u32[]{:S(2)}) collective-permute-start(s32[1]{0:T(128)} %param.13), channel_id=1, source_target_pairs={{0,1},{1,2},{2,3},{3,4},{4,5},{5,6},{6,7},{7,8},{8,9},{9,10},{10,1... | collective-permute-start | bytes 20 | tf_op jit(solution)/shard_map/ppermute | solution.py:17
  20.4 7.0 %collective-permute-done.4 = s32[1]{0:T(128)} collective-permute-done((s32[1]{0:T(128)}, s32[1]{0:T(128)}, u32[]{:S(2)}, u32[]{:S(2)}) %collective-permute-start.4) | collective-permute-done | bytes 36 | tf_op jit(solution)/shard_map/ppermute | solution.py:17
  28.1 0.0 collective-permute-done.5.kv_ref
  28.1 0.0 copy-start.5
  28.1 0.7 copy-done.5
  28.8 0.0 copy-start.3
  28.8 8.2 %shard_map.95 = (f32[512,1024]{1,0:T(8,128)}, f32[512,256]{1,0:T(8,128)}) custom-call(s32[1]{0:T(128)S(6)} %select_n.15.info_ref, bf16[512,1024]{1,0:T(8,128)(2,1)} %q_ref.7, bf16[512,1024]{1,0:T(8,128)(2,1)} %do_ref.7, bf16[512,256]{1,0:T(8,128)(2,1)} %copy-done.5, f32[8,512]{1,0:T(8,128)} %lse_ref.7, ...), custom_call_target="tpu_custom_call", output_to_operand_aliasing={{0}: (6, {})} | custom-call | flops 1342177280 | bytes 6553600 | tf_op jit(solution)/shard_map/pallas_call | solution.py:102
  37.0 0.0 collective-permute-done.6
  37.0 1.1 %add.9 = f32[512,256]{1,0:T(8,128)S(1)} add(f32[512,256]{1,0:T(8,128)S(1)} %collective-permute-done.6, f32[512,256]{1,0:T(8,128)} %get-tuple-element.16) | non-fusion elementwise | flops 131072 | bytes 1572864 | tf_op jit(solution)/shard_map/add | solution.py:153
  38.1 2.5 %collective-permute-start.7 = (f32[512,256]{1,0:T(8,128)S(1)}, f32[512,256]{1,0:T(8,128)S(1)}, u32[]{:S(2)}, u32[]{:S(2)}) collective-permute-start(f32[512,256]{1,0:T(8,128)S(1)} %add.9), channel_id=1, source_target_pairs={{0,1},{1,2},{2,3},{3,4},{4,5},{5,6},{6,7},{7,8},{8,9},{9,10},{10,1... | collective-permute-start | bytes 1572872 | tf_op jit(solution)/shard_map/ppermute | solution.py:17
  40.6 0.0 copy-done.3
  40.6 1.2 %collective-permute-start.3 = (bf16[512,256]{1,0:T(8,128)(2,1)S(1)}, bf16[512,256]{1,0:T(8,128)(2,1)S(1)}, u32[]{:S(2)}, u32[]{:S(2)}) collective-permute-start(bf16[512,256]{1,0:T(8,128)(2,1)S(1)} %copy-done.3), channel_id=1, source_target_pairs={{0,2},{1,3},{2,4},{3,5},{4,6},{5,7},{6,8},{7,9},{8,10},{9,11},{10,... | collective-permute-start | bytes 786440 | tf_op jit(solution)/shard_map/ppermute | solution.py:17
  41.8 0.9 collective-permute-start.2
  42.7 24.0 %collective-permute-done.2 = s32[1]{0:T(128)} collective-permute-done((s32[1]{0:T(128)}, s32[1]{0:T(128)}, u32[]{:S(2)}, u32[]{:S(2)}) %collective-permute-start.2) | collective-permute-done | bytes 36 | tf_op jit(solution)/shard_map/ppermute | solution.py:17
  67.4 0.0 collective-permute-done.3.kv_ref
  67.4 0.0 copy-start.6
  67.4 0.7 copy-done.6
  68.1 8.1 %shard_map.96 = (f32[512,1024]{1,0:T(8,128)}, f32[512,256]{1,0:T(8,128)}) custom-call(s32[1]{0:T(128)S(6)} %select_n.14.info_ref, bf16[512,1024]{1,0:T(8,128)(2,1)} %q_ref.7, bf16[512,1024]{1,0:T(8,128)(2,1)} %do_ref.7, bf16[512,256]{1,0:T(8,128)(2,1)} %copy-done.6, f32[8,512]{1,0:T(8,128)} %lse_ref.7, ...), custom_call_target="tpu_custom_call", output_to_operand_aliasing={{0}: (6, {})} | custom-call | flops 1342177280 | bytes 6553600 | tf_op jit(solution)/shard_map/pallas_call | solution.py:102
  76.2 0.0 collective-permute-done.7
  76.3 1.1 %add.10 = f32[512,256]{1,0:T(8,128)S(1)} add(f32[512,256]{1,0:T(8,128)S(1)} %collective-permute-done.7, f32[512,256]{1,0:T(8,128)} %get-tuple-element.17) | non-fusion elementwise | flops 131072 | bytes 1572864 | tf_op jit(solution)/shard_map/add | solution.py:153
  77.4 0.1 collective-permute-start.8
  77.5 0.1 collective-permute-start.1
  77.5 0.1 collective-permute-start
  77.6 14.6 %collective-permute-done = s32[1]{0:T(128)} collective-permute-done((s32[1]{0:T(128)}, s32[1]{0:T(128)}, u32[]{:S(2)}, u32[]{:S(2)}) %collective-permute-start) | collective-permute-done | bytes 36 | tf_op jit(solution)/shard_map/ppermute | solution.py:17
  92.9 0.0 collective-permute-done.1.kv_ref
  92.9 0.0 copy-start.4
  92.9 0.7 copy-done.4
  93.6 7.9 %shard_map.97 = (bf16[512,1024]{1,0:T(8,128)(2,1)}, f32[512,256]{1,0:T(8,128)}) custom-call(s32[1]{0:T(128)S(6)} %select_n.13.info_ref, bf16[512,1024]{1,0:T(8,128)(2,1)} %q_ref.7, bf16[512,1024]{1,0:T(8,128)(2,1)} %do_ref.7, bf16[512,256]{1,0:T(8,128)(2,1)} %copy-done.4, f32[8,512]{1,0:T(8,128)} %lse_ref.7, f32[8,512]{1,0:T(8,128)} %copy.18.dl_ref, ...), custom_call_target="tpu_custom_call" | custom-call | flops 1342177280 | bytes 6553600 | tf_op jit(solution)/shard_map/pallas_call | solution.py:102
  101.5 0.0 collective-permute-done.8
  101.5 1.1 add_convert_fusion
  102.6 0.1 collective-permute-start.9
  102.7 7.3 %collective-permute-done.9 = bf16[512,256]{1,0:T(8,128)(2,1)S(1)} collective-permute-done((bf16[512,256]{1,0:T(8,128)(2,1)S(1)}, bf16[512,256]{1,0:T(8,128)(2,1)S(1)}, u32[]{:S(2)}, u32[]{:S(2)}) %collective-permute-start.9) | collective-permute-done | bytes 262176 | tf_op jit(solution)/shard_map/ppermute | solution.py:17
  110.0 0.7 fusion.1
  (1 shorter events, 0.0 us)
Async XLA Ops:
  0.6 2.5 %copy-start = (bf16[512,1024]{1,0:T(8,128)(2,1)S(1)}, bf16[512,1024]{1,0:T(8,128)(2,1)}, u32[]{:S(2)}) copy-start(bf16[512,1024]{1,0:T(8,128)(2,1)} %do_ref.7) | copy-start | bytes 3145732
  3.2 1.6 %copy-start.1 = (bf16[512,128]{1,0:T(8,128)(2,1)S(1)}, bf16[512,128]{1,0:T(8,128)(2,1)}, u32[]{:S(2)}) copy-start(bf16[512,128]{1,0:T(8,128)(2,1)} %param.9) | copy-start | bytes 393220
  4.9 0.7 copy-start.2
  15.5 21.4 %collective-permute-start.6 = (f32[512,256]{1,0:T(8,128)}, f32[512,256]{1,0:T(8,128)S(1)}, u32[]{:S(2)}, u32[]{:S(2)}) collective-permute-start(f32[512,256]{1,0:T(8,128)} %get-tuple-element.15), channel_id=1, source_target_pairs={{0,1},{1,2},{2,3},{3,4},{4,5},{5,6},{6,7},{7,8},{8,9},{9,10},{10,1... | collective-permute-start | bytes 1572872 | tf_op jit(solution)/shard_map/ppermute | solution.py:17
  18.1 9.9 %collective-permute-start.5 = (bf16[512,256]{1,0:T(8,128)(2,1)}, bf16[512,256]{1,0:T(8,128)(2,1)S(1)}, u32[]{:S(2)}, u32[]{:S(2)}) collective-permute-start(bf16[512,256]{1,0:T(8,128)(2,1)} %copy-done.2), channel_id=1, source_target_pairs={{0,1},{1,2},{2,3},{3,4},{4,5},{5,6},{6,7},{7,8},{8,9},{9,10},{10,1... | collective-permute-start | bytes 786440 | tf_op jit(solution)/shard_map/ppermute | solution.py:17
  18.2 9.2 %collective-permute-start.4 = (s32[1]{0:T(128)}, s32[1]{0:T(128)}, u32[]{:S(2)}, u32[]{:S(2)}) collective-permute-start(s32[1]{0:T(128)} %param.13), channel_id=1, source_target_pairs={{0,1},{1,2},{2,3},{3,4},{4,5},{5,6},{6,7},{7,8},{8,9},{9,10},{10,1... | collective-permute-start | bytes 20 | tf_op jit(solution)/shard_map/ppermute | solution.py:17
  28.1 0.7 copy-start.5
  28.8 11.8 %copy-start.3 = (bf16[512,256]{1,0:T(8,128)(2,1)S(1)}, bf16[512,256]{1,0:T(8,128)(2,1)}, u32[]{:S(2)}) copy-start(bf16[512,256]{1,0:T(8,128)(2,1)} %copy-done.2) | copy-start | bytes 786436
  38.1 38.2 %collective-permute-start.7 = (f32[512,256]{1,0:T(8,128)S(1)}, f32[512,256]{1,0:T(8,128)S(1)}, u32[]{:S(2)}, u32[]{:S(2)}) collective-permute-start(f32[512,256]{1,0:T(8,128)S(1)} %add.9), channel_id=1, source_target_pairs={{0,1},{1,2},{2,3},{3,4},{4,5},{5,6},{6,7},{7,8},{8,9},{9,10},{10,1... | collective-permute-start | bytes 1572872 | tf_op jit(solution)/shard_map/ppermute | solution.py:17
  40.6 26.8 %collective-permute-start.3 = (bf16[512,256]{1,0:T(8,128)(2,1)S(1)}, bf16[512,256]{1,0:T(8,128)(2,1)S(1)}, u32[]{:S(2)}, u32[]{:S(2)}) collective-permute-start(bf16[512,256]{1,0:T(8,128)(2,1)S(1)} %copy-done.3), channel_id=1, source_target_pairs={{0,2},{1,3},{2,4},{3,5},{4,6},{5,7},{6,8},{7,9},{8,10},{9,11},{10,... | collective-permute-start | bytes 786440 | tf_op jit(solution)/shard_map/ppermute | solution.py:17
  41.8 24.9 %collective-permute-start.2 = (s32[1]{0:T(128)}, s32[1]{0:T(128)}, u32[]{:S(2)}, u32[]{:S(2)}) collective-permute-start(s32[1]{0:T(128)} %param.13), channel_id=1, source_target_pairs={{0,2},{1,3},{2,4},{3,5},{4,6},{5,7},{6,8},{7,9},{8,10},{9,11},{10,... | collective-permute-start | bytes 20 | tf_op jit(solution)/shard_map/ppermute | solution.py:17
  67.4 0.7 copy-start.6
  77.4 24.2 %collective-permute-start.8 = (f32[512,256]{1,0:T(8,128)S(1)}, f32[512,256]{1,0:T(8,128)S(1)}, u32[]{:S(2)}, u32[]{:S(2)}) collective-permute-start(f32[512,256]{1,0:T(8,128)S(1)} %add.10), channel_id=1, source_target_pairs={{0,1},{1,2},{2,3},{3,4},{4,5},{5,6},{6,7},{7,8},{8,9},{9,10},{10,1... | collective-permute-start | bytes 1572872 | tf_op jit(solution)/shard_map/ppermute | solution.py:17
  77.5 15.4 %collective-permute-start.1 = (bf16[512,256]{1,0:T(8,128)(2,1)S(1)}, bf16[512,256]{1,0:T(8,128)(2,1)S(1)}, u32[]{:S(2)}, u32[]{:S(2)}) collective-permute-start(bf16[512,256]{1,0:T(8,128)(2,1)S(1)} %copy-done.3), channel_id=1, source_target_pairs={{0,3},{1,4},{2,5},{3,6},{4,7},{5,8},{6,9},{7,10},{8,11},{9,12},{10... | collective-permute-start | bytes 786440 | tf_op jit(solution)/shard_map/ppermute | solution.py:17
  77.5 14.6 %collective-permute-start = (s32[1]{0:T(128)}, s32[1]{0:T(128)}, u32[]{:S(2)}, u32[]{:S(2)}) collective-permute-start(s32[1]{0:T(128)} %param.13), channel_id=1, source_target_pairs={{0,3},{1,4},{2,5},{3,6},{4,7},{5,8},{6,9},{7,10},{8,11},{9,12},{10... | collective-permute-start | bytes 20 | tf_op jit(solution)/shard_map/ppermute | solution.py:17
  92.9 0.7 copy-start.4
  102.6 7.4 %collective-permute-start.9 = (bf16[512,256]{1,0:T(8,128)(2,1)S(1)}, bf16[512,256]{1,0:T(8,128)(2,1)S(1)}, u32[]{:S(2)}, u32[]{:S(2)}) collective-permute-start(bf16[512,256]{1,0:T(8,128)(2,1)S(1)} %add_convert_fusion), channel_id=1, source_target_pairs={{0,253},{1,254},{2,255},{3,0},{4,1},{5,2},{6,3},{7,4},{8,5},{9,6},... | collective-permute-start | bytes 786440 | tf_op jit(solution)/shard_map/ppermute | solution.py:17

commit v2 on v0

v2 whole, which is shorter than its diff:
```python
import functools

import jax
import jax.numpy as jnp
from jax import lax
from jax.experimental import pallas as pl
from jax.experimental.pallas import tpu as pltpu
from jax.sharding import PartitionSpec as P


STEPS = 4


def passed_along(value, axis, steps):
    count = lax.axis_size(axis)
    pairs = [(source, (source + steps) % count) for source in range(count)]
    return lax.ppermute(value, axis, pairs)


def tile_body(tiles, has_in, group, half, width, scale,
              info_ref, q_ref, do_ref, kv_ref, lse_ref, dl_ref, *rest):
    if has_in:
        dqin_ref, dq_ref, dkv_ref, acc_ref = rest
    else:
        dq_ref, dkv_ref, acc_ref = rest
    block = pl.program_id(0)

    @pl.when(block == 0)
    def _():
        dkv_ref[...] = jnp.zeros_like(dkv_ref)

    if has_in:
        acc_ref[...] = dqin_ref[...]
    else:
        acc_ref[...] = jnp.zeros_like(acc_ref)
    other = info_ref[0]
    lse_all = [lse_ref[pl.ds(block * group + j, 1), :] for j in range(group)]
    dl_all = [dl_ref[pl.ds(block * group + j, 1), :] for j in range(group)]
    for q_sel, k_sel, diag in tiles:
        if q_sel is None:
            qi = other
            lse = jnp.concatenate(
                [jnp.where(other == 0, x[:, :half], x[:, half:]) for x in lse_all], axis=1)
            dl = jnp.concatenate(
                [jnp.where(other == 0, x[:, :half], x[:, half:]) for x in dl_all], axis=1)
        else:
            qi = q_sel
            lanes = slice(q_sel * half, (q_sel + 1) * half)
            lse = jnp.concatenate([x[:, lanes] for x in lse_all], axis=1)
            dl = jnp.concatenate([x[:, lanes] for x in dl_all], axis=1)
        ki = other if k_sel is None else k_sel
        q_rows = pl.ds(pl.multiple_of(qi * half, half), half)
        k_rows = pl.ds(pl.multiple_of(ki * half, half), half)
        q = jnp.concatenate(
            [q_ref[q_rows, pl.ds(j * width, width)] for j in range(group)], axis=0)
        do = jnp.concatenate(
            [do_ref[q_rows, pl.ds(j * width, width)] for j in range(group)], axis=0)
        k = kv_ref[k_rows, pl.ds(0, width)]
        v = kv_ref[k_rows, pl.ds(width, width)]
        s_t = lax.dot_general(k, q, (((1,), (1,)), ((), ())),
                              preferred_element_type=jnp.float32) * scale
        p_t = jnp.exp(s_t - lse)
        if diag:
            rows = lax.broadcasted_iota(jnp.int32, (half, group * half), 0)
            cols_i = lax.broadcasted_iota(jnp.int32, (half, group * half), 1) % half
            p_t = jnp.where(rows <= cols_i, p_t, 0.0)
        dp_t = lax.dot_general(v, do, (((1,), (1,)), ((), ())),
                               preferred_element_type=jnp.float32)
        ds_t = (p_t * (dp_t - dl) * scale).astype(jnp.bfloat16)
        pb_t = p_t.astype(jnp.bfloat16)
        dv = jnp.dot(pb_t, do, preferred_element_type=jnp.float32)
        dk = jnp.dot(ds_t, q, preferred_element_type=jnp.float32)
        dq = lax.dot_general(ds_t, k, (((0,), (0,)), ((), ())),
                             preferred_element_type=jnp.float32)
        for j in range(group):
            acc_ref[q_rows, pl.ds(j * width, width)] += dq[j * half:(j + 1) * half]
        dkv_ref[k_rows, pl.ds(0, width)] += dk
        dkv_ref[k_rows, pl.ds(width, width)] += dv
    dq_ref[...] = acc_ref[...].astype(dq_ref.dtype)


GROUP = 4


def tile_step(tiles, info, queries, grad_out, kv, lse, delta, dq_in, dq_dtype):
    rows, cols = queries.shape
    width = kv.shape[1] // 2
    heads = cols // width
    half = rows // 2
    scale = width ** (-0.5)
    has_in = dq_in is not None
    col_spec = pl.BlockSpec((rows, GROUP * width), lambda g, info: (0, g))
    kv_spec = pl.BlockSpec((rows, 2 * width), lambda g, info: (0, 0))
    row_spec = pl.BlockSpec((heads, rows), lambda g, info: (0, 0))
    in_specs = [col_spec, col_spec, kv_spec, row_spec, row_spec]
    args = [queries, grad_out, kv, lse, delta]
    aliases = {}
    if has_in:
        in_specs.append(col_spec)
        args.append(dq_in)
        if dq_in.dtype == dq_dtype:
            aliases = {len(args): 0}
    flops = len(tiles) * heads * 5 * 2 * half * half * width
    nbytes = 2 * rows * cols * 2 + rows * 2 * width * 2 + rows * cols * 4 * (2 if has_in else 1)
    return pl.pallas_call(
        functools.partial(tile_body, tiles, has_in, GROUP, half, width, scale),
        out_shape=(
            jax.ShapeDtypeStruct((rows, cols), dq_dtype),
            jax.ShapeDtypeStruct((rows, 2 * width), jnp.float32),
        ),
        grid_spec=pltpu.PrefetchScalarGridSpec(
            num_scalar_prefetch=1,
            grid=(heads // GROUP,),
            in_specs=in_specs,
            out_specs=[col_spec, kv_spec],
            scratch_shapes=[pltpu.VMEM((rows, GROUP * width), jnp.float32)],
        ),
        input_output_aliases=aliases,
        compiler_params=pltpu.CompilerParams(dimension_semantics=("arbitrary",)),
        cost_estimate=pl.CostEstimate(
            flops=flops, transcendentals=len(tiles) * heads * half * half, bytes_accessed=nbytes
        ),
    )(info, *args)


OWN_TILES = ((0, 0, True), (1, 0, False), (1, 1, True))
VISIT_TILES = ((1, 0, False), (None, None, False))


def device_steps(queries, key_rows, value_rows, grad_out, attn_out, log_total, block_pair):
    rows, width = key_rows.shape
    heads = queries.shape[1] // width
    own_block = block_pair[0]
    kv = jnp.concatenate([key_rows, value_rows], axis=1)
    delta = jnp.einsum(
        "qhd,qhd->hq",
        grad_out.reshape(rows, heads, width),
        attn_out.reshape(rows, heads, width),
        preferred_element_type=jnp.float32,
    )

    visitors = [(kv, block_pair)]
    for step in range(1, STEPS):
        visitors.append(passed_along((kv, block_pair), "ctx", step))

    zero_info = jnp.zeros((1,), jnp.int32)
    dq, sums = tile_step(OWN_TILES, zero_info, queries, grad_out, kv, log_total, delta,
                         None, jnp.float32)
    for step in range(1, STEPS):
        received = passed_along(sums, "ctx", 1)
        kv_s, block_s = visitors[step]
        other = jnp.where(block_s[0] < own_block, 0, 1).astype(jnp.int32).reshape(1)
        last = step == STEPS - 1
        dq, part = tile_step(VISIT_TILES, other, queries, grad_out, kv_s, log_total, delta,
                             dq, jnp.bfloat16 if last else jnp.float32)
        sums = received + part
    final = passed_along(sums.astype(jnp.bfloat16), "ctx", 1 - STEPS)
    return dq, final[:, :width], final[:, width:]


def solution(mesh):
    return jax.shard_map(
        device_steps,
        mesh=mesh,
        in_specs=(
            P("ctx", None),
            P("ctx", None),
            P("ctx", None),
            P("ctx", None),
            P("ctx", None),
            P(None, "ctx"),
            P("ctx"),
        ),
        out_specs=(P("ctx", None), P("ctx", None), P("ctx", None)),
        check_vma=False,
    )
```

time: 113 us -> 103 us (0.912)
  the two profiles are of different devices: /device:TPU:125 before, /device:TPU:1 now
where the time goes in v2:
time: 103 us
  waiting for transfers between devices  52.9 us (51%)
  Pallas kernels  26 us (25%)
  starting transfers between devices  9.32 us (9%)
  local copies, waits for them, and re-layouts  7.06 us (7%)
  other arithmetic  3.95 us (4%)
  between operations  3.53 us (3%)
    ppermute x10, waiting for transfers between devices, passed_along(): return lax.ppermute(value, axis, pairs)  52.9 us
    pallas_call x4, Pallas kernels, tile_step(): pl.pallas_call(functools.partial(tile_body, tiles, has_in, GROUP, half, w...  26 us
    ppermute x10, starting transfers between devices, passed_along(): return lax.ppermute(value, axis, pairs)  9.32 us
    unnamed x17, local copies, waits for them, and re-layouts  5.6 us
    add x2, other arithmetic, device_steps(): sums = received + part  2.22 us
  transfers between devices with their start and end apart: 10, of which 4 were waited for; matrix products, arithmetic and copies ran while one was open for 0% of the time, Pallas kernels for 18%

profile of v2, /device:TPU:1, one launch (start us, length us, event | category | flops | bytes accessed | tf_op | source)
XLA Modules:
  0.0 102.7 jit_solution(1637636815240303208)
XLA Ops:
  0.6 0.0 copy-start
  0.6 1.0 constant_dynamic-update-slice_fusion.1
  1.7 1.5 %copy.21 = bf16[64,8,8,128]{3,2,1,0:T(8,128)(2,1)S(1)} copy(bf16[64,8,8,128]{3,1,2,0:T(8,128)(2,1)} %bitcast.10) | data formatting | bytes 2097152
  3.2 0.0 copy-done
  3.2 0.0 copy-start.1
  3.2 0.3 copy.20
  3.5 0.6 fusion
  4.1 0.7 copy.18.dl_ref
  4.8 0.0 copy-done.1
  4.9 0.0 copy-start.2
  4.9 0.7 copy-done.2
  5.6 7.2 %shard_map.94 = (f32[512,1024]{1,0:T(8,128)}, f32[512,256]{1,0:T(8,128)}) custom-call(s32[1]{0:T(128)} %constant.9.clone.1.info_ref, bf16[512,1024]{1,0:T(8,128)(2,1)} %q_ref.7, bf16[512,1024]{1,0:T(8,128)(2,1)} %do_ref.7, bf16[512,256]{1,0:T(8,128)(2,1)} %copy-done.2, f32[8,512]{1,0:T(8,128)} %lse_ref.7, f32[8,512]{1,0:T(8,128)} %copy.18.dl_ref), custom_call_target="tpu_custom_call" | custom-call | flops 2013265920 | bytes 4456448 | tf_op jit(solution)/shard_map/pallas_call | solution.py:105
  12.8 2.6 %collective-permute-start.6 = (f32[512,256]{1,0:T(8,128)}, f32[512,256]{1,0:T(8,128)S(1)}, u32[]{:S(2)}, u32[]{:S(2)}) collective-permute-start(f32[512,256]{1,0:T(8,128)} %get-tuple-element.15), channel_id=1, source_target_pairs={{0,1},{1,2},{2,3},{3,4},{4,5},{5,6},{6,7},{7,8},{8,9},{9,10},{10,1... | collective-permute-start | bytes 1572872 | tf_op jit(solution)/shard_map/ppermute | solution.py:17
  15.4 0.0 collective-permute-start.5
  15.4 1.6 %collective-permute-start.4 = (s32[1]{0:T(128)}, s32[1]{0:T(128)}, u32[]{:S(2)}, u32[]{:S(2)}) collective-permute-start(s32[1]{0:T(128)} %param.13), channel_id=1, source_target_pairs={{0,1},{1,2},{2,3},{3,4},{4,5},{5,6},{6,7},{7,8},{8,9},{9,10},{10,1... | collective-permute-start | bytes 20 | tf_op jit(solution)/shard_map/ppermute | solution.py:17
  17.7 7.0 %collective-permute-done.4 = s32[1]{0:T(128)} collective-permute-done((s32[1]{0:T(128)}, s32[1]{0:T(128)}, u32[]{:S(2)}, u32[]{:S(2)}) %collective-permute-start.4) | collective-permute-done | bytes 36 | tf_op jit(solution)/shard_map/ppermute | solution.py:17
  25.3 0.0 collective-permute-done.5.kv_ref
  25.4 0.0 copy-start.5
  25.4 0.7 copy-done.5
  26.0 0.0 copy-start.3
  26.0 6.4 %shard_map.95 = (f32[512,1024]{1,0:T(8,128)}, f32[512,256]{1,0:T(8,128)}) custom-call(s32[1]{0:T(128)S(6)} %select_n.15.info_ref, bf16[512,1024]{1,0:T(8,128)(2,1)} %q_ref.7, bf16[512,1024]{1,0:T(8,128)(2,1)} %do_ref.7, bf16[512,256]{1,0:T(8,128)(2,1)} %copy-done.5, f32[8,512]{1,0:T(8,128)} %lse_ref.7, ...), custom_call_target="tpu_custom_call", output_to_operand_aliasing={{0}: (6, {})} | custom-call | flops 1342177280 | bytes 6553600 | tf_op jit(solution)/shard_map/pallas_call | solution.py:105
  32.4 0.0 collective-permute-done.6
  32.4 1.1 %add.9 = f32[512,256]{1,0:T(8,128)S(1)} add(f32[512,256]{1,0:T(8,128)S(1)} %collective-permute-done.6, f32[512,256]{1,0:T(8,128)} %get-tuple-element.16) | non-fusion elementwise | flops 131072 | bytes 1572864 | tf_op jit(solution)/shard_map/add | solution.py:156
  33.5 2.5 %collective-permute-start.7 = (f32[512,256]{1,0:T(8,128)S(1)}, f32[512,256]{1,0:T(8,128)S(1)}, u32[]{:S(2)}, u32[]{:S(2)}) collective-permute-start(f32[512,256]{1,0:T(8,128)S(1)} %add.9), channel_id=1, source_target_pairs={{0,1},{1,2},{2,3},{3,4},{4,5},{5,6},{6,7},{7,8},{8,9},{9,10},{10,1... | collective-permute-start | bytes 1572872 | tf_op jit(solution)/shard_map/ppermute | solution.py:17
  36.0 0.0 copy-done.3
  36.0 1.2 %collective-permute-start.3 = (bf16[512,256]{1,0:T(8,128)(2,1)S(1)}, bf16[512,256]{1,0:T(8,128)(2,1)S(1)}, u32[]{:S(2)}, u32[]{:S(2)}) collective-permute-start(bf16[512,256]{1,0:T(8,128)(2,1)S(1)} %copy-done.3), channel_id=1, source_target_pairs={{0,2},{1,3},{2,4},{3,5},{4,6},{5,7},{6,8},{7,9},{8,10},{9,11},{10,... | collective-permute-start | bytes 786440 | tf_op jit(solution)/shard_map/ppermute | solution.py:17
  37.2 0.9 collective-permute-start.2
  38.1 24.1 %collective-permute-done.2 = s32[1]{0:T(128)} collective-permute-done((s32[1]{0:T(128)}, s32[1]{0:T(128)}, u32[]{:S(2)}, u32[]{:S(2)}) %collective-permute-start.2) | collective-permute-done | bytes 36 | tf_op jit(solution)/shard_map/ppermute | solution.py:17
  62.9 0.0 collective-permute-done.3.kv_ref
  62.9 0.0 copy-start.6
  62.9 0.7 copy-done.6
  63.6 6.3 %shard_map.96 = (f32[512,1024]{1,0:T(8,128)}, f32[512,256]{1,0:T(8,128)}) custom-call(s32[1]{0:T(128)S(6)} %select_n.14.info_ref, bf16[512,1024]{1,0:T(8,128)(2,1)} %q_ref.7, bf16[512,1024]{1,0:T(8,128)(2,1)} %do_ref.7, bf16[512,256]{1,0:T(8,128)(2,1)} %copy-done.6, f32[8,512]{1,0:T(8,128)} %lse_ref.7, ...), custom_call_target="tpu_custom_call", output_to_operand_aliasing={{0}: (6, {})} | custom-call | flops 1342177280 | bytes 6553600 | tf_op jit(solution)/shard_map/pallas_call | solution.py:105
  69.9 0.0 collective-permute-done.7
  69.9 1.1 %add.10 = f32[512,256]{1,0:T(8,128)S(1)} add(f32[512,256]{1,0:T(8,128)S(1)} %collective-permute-done.7, f32[512,256]{1,0:T(8,128)} %get-tuple-element.17) | non-fusion elementwise | flops 131072 | bytes 1572864 | tf_op jit(solution)/shard_map/add | solution.py:156
  71.0 0.3 collective-permute-start.8
  71.3 0.1 collective-permute-start.1
  71.3 0.1 collective-permute-start
  71.4 14.6 %collective-permute-done = s32[1]{0:T(128)} collective-permute-done((s32[1]{0:T(128)}, s32[1]{0:T(128)}, u32[]{:S(2)}, u32[]{:S(2)}) %collective-permute-start) | collective-permute-done | bytes 36 | tf_op jit(solution)/shard_map/ppermute | solution.py:17
  86.7 0.0 collective-permute-done.1.kv_ref
  86.7 0.0 copy-start.4
  86.7 0.7 copy-done.4
  87.4 6.1 %shard_map.97 = (bf16[512,1024]{1,0:T(8,128)(2,1)}, f32[512,256]{1,0:T(8,128)}) custom-call(s32[1]{0:T(128)S(6)} %select_n.13.info_ref, bf16[512,1024]{1,0:T(8,128)(2,1)} %q_ref.7, bf16[512,1024]{1,0:T(8,128)(2,1)} %do_ref.7, bf16[512,256]{1,0:T(8,128)(2,1)} %copy-done.4, f32[8,512]{1,0:T(8,128)} %lse_ref.7, f32[8,512]{1,0:T(8,128)} %copy.18.dl_ref, ...), custom_call_target="tpu_custom_call" | custom-call | flops 1342177280 | bytes 6553600 | tf_op jit(solution)/shard_map/pallas_call | solution.py:105
  93.5 0.0 collective-permute-done.8
  93.5 1.1 %add_convert_fusion = bf16[512,256]{1,0:T(8,128)(2,1)S(1)} fusion(f32[512,256]{1,0:T(8,128)S(1)} %collective-permute-done.8, f32[512,256]{1,0:T(8,128)} %get-tuple-element.18), kind=kLoop, calls=%fused_computation.2 | loop fusion | flops 262144 | bytes 1310720 | tf_op jit(solution)/shard_map/convert_element_type | solution.py:157
  94.6 0.1 collective-permute-start.9
  94.7 7.3 %collective-permute-done.9 = bf16[512,256]{1,0:T(8,128)(2,1)S(1)} collective-permute-done((bf16[512,256]{1,0:T(8,128)(2,1)S(1)}, bf16[512,256]{1,0:T(8,128)(2,1)S(1)}, u32[]{:S(2)}, u32[]{:S(2)}) %collective-permute-start.9) | collective-permute-done | bytes 262176 | tf_op jit(solution)/shard_map/ppermute | solution.py:17
  102.0 0.7 fusion.1
  (1 shorter events, 0.0 us)
Async XLA Ops:
  0.6 2.5 %copy-start = (bf16[512,1024]{1,0:T(8,128)(2,1)S(1)}, bf16[512,1024]{1,0:T(8,128)(2,1)}, u32[]{:S(2)}) copy-start(bf16[512,1024]{1,0:T(8,128)(2,1)} %do_ref.7) | copy-start | bytes 3145732
  3.2 1.6 %copy-start.1 = (bf16[512,128]{1,0:T(8,128)(2,1)S(1)}, bf16[512,128]{1,0:T(8,128)(2,1)}, u32[]{:S(2)}) copy-start(bf16[512,128]{1,0:T(8,128)(2,1)} %param.9) | copy-start | bytes 393220
  4.9 0.7 copy-start.2
  12.8 19.6 %collective-permute-start.6 = (f32[512,256]{1,0:T(8,128)}, f32[512,256]{1,0:T(8,128)S(1)}, u32[]{:S(2)}, u32[]{:S(2)}) collective-permute-start(f32[512,256]{1,0:T(8,128)} %get-tuple-element.15), channel_id=1, source_target_pairs={{0,1},{1,2},{2,3},{3,4},{4,5},{5,6},{6,7},{7,8},{8,9},{9,10},{10,1... | collective-permute-start | bytes 1572872 | tf_op jit(solution)/shard_map/ppermute | solution.py:17
  15.4 9.9 %collective-permute-start.5 = (bf16[512,256]{1,0:T(8,128)(2,1)}, bf16[512,256]{1,0:T(8,128)(2,1)S(1)}, u32[]{:S(2)}, u32[]{:S(2)}) collective-permute-start(bf16[512,256]{1,0:T(8,128)(2,1)} %copy-done.2), channel_id=1, source_target_pairs={{0,1},{1,2},{2,3},{3,4},{4,5},{5,6},{6,7},{7,8},{8,9},{9,10},{10,1... | collective-permute-start | bytes 786440 | tf_op jit(solution)/shard_map/ppermute | solution.py:17
  15.4 9.2 %collective-permute-start.4 = (s32[1]{0:T(128)}, s32[1]{0:T(128)}, u32[]{:S(2)}, u32[]{:S(2)}) collective-permute-start(s32[1]{0:T(128)} %param.13), channel_id=1, source_target_pairs={{0,1},{1,2},{2,3},{3,4},{4,5},{5,6},{6,7},{7,8},{8,9},{9,10},{10,1... | collective-permute-start | bytes 20 | tf_op jit(solution)/shard_map/ppermute | solution.py:17
  25.4 0.7 copy-start.5
  26.0 10.0 %copy-start.3 = (bf16[512,256]{1,0:T(8,128)(2,1)S(1)}, bf16[512,256]{1,0:T(8,128)(2,1)}, u32[]{:S(2)}) copy-start(bf16[512,256]{1,0:T(8,128)(2,1)} %copy-done.2) | copy-start | bytes 786436
  33.5 36.4 %collective-permute-start.7 = (f32[512,256]{1,0:T(8,128)S(1)}, f32[512,256]{1,0:T(8,128)S(1)}, u32[]{:S(2)}, u32[]{:S(2)}) collective-permute-start(f32[512,256]{1,0:T(8,128)S(1)} %add.9), channel_id=1, source_target_pairs={{0,1},{1,2},{2,3},{3,4},{4,5},{5,6},{6,7},{7,8},{8,9},{9,10},{10,1... | collective-permute-start | bytes 1572872 | tf_op jit(solution)/shard_map/ppermute | solution.py:17
  36.0 26.9 %collective-permute-start.3 = (bf16[512,256]{1,0:T(8,128)(2,1)S(1)}, bf16[512,256]{1,0:T(8,128)(2,1)S(1)}, u32[]{:S(2)}, u32[]{:S(2)}) collective-permute-start(bf16[512,256]{1,0:T(8,128)(2,1)S(1)} %copy-done.3), channel_id=1, source_target_pairs={{0,2},{1,3},{2,4},{3,5},{4,6},{5,7},{6,8},{7,9},{8,10},{9,11},{10,... | collective-permute-start | bytes 786440 | tf_op jit(solution)/shard_map/ppermute | solution.py:17
  37.2 25.0 %collective-permute-start.2 = (s32[1]{0:T(128)}, s32[1]{0:T(128)}, u32[]{:S(2)}, u32[]{:S(2)}) collective-permute-start(s32[1]{0:T(128)} %param.13), channel_id=1, source_target_pairs={{0,2},{1,3},{2,4},{3,5},{4,6},{5,7},{6,8},{7,9},{8,10},{9,11},{10,... | collective-permute-start | bytes 20 | tf_op jit(solution)/shard_map/ppermute | solution.py:17
  62.9 0.7 copy-start.6
  71.0 22.5 %collective-permute-start.8 = (f32[512,256]{1,0:T(8,128)S(1)}, f32[512,256]{1,0:T(8,128)S(1)}, u32[]{:S(2)}, u32[]{:S(2)}) collective-permute-start(f32[512,256]{1,0:T(8,128)S(1)} %add.10), channel_id=1, source_target_pairs={{0,1},{1,2},{2,3},{3,4},{4,5},{5,6},{6,7},{7,8},{8,9},{9,10},{10,1... | collective-permute-start | bytes 1572872 | tf_op jit(solution)/shard_map/ppermute | solution.py:17
  71.3 15.4 %collective-permute-start.1 = (bf16[512,256]{1,0:T(8,128)(2,1)S(1)}, bf16[512,256]{1,0:T(8,128)(2,1)S(1)}, u32[]{:S(2)}, u32[]{:S(2)}) collective-permute-start(bf16[512,256]{1,0:T(8,128)(2,1)S(1)} %copy-done.3), channel_id=1, source_target_pairs={{0,3},{1,4},{2,5},{3,6},{4,7},{5,8},{6,9},{7,10},{8,11},{9,12},{10... | collective-permute-start | bytes 786440 | tf_op jit(solution)/shard_map/ppermute | solution.py:17
  71.3 14.7 %collective-permute-start = (s32[1]{0:T(128)}, s32[1]{0:T(128)}, u32[]{:S(2)}, u32[]{:S(2)}) collective-permute-start(s32[1]{0:T(128)} %param.13), channel_id=1, source_target_pairs={{0,3},{1,4},{2,5},{3,6},{4,7},{5,8},{6,9},{7,10},{8,11},{9,12},{10... | collective-permute-start | bytes 20 | tf_op jit(solution)/shard_map/ppermute | solution.py:17
  86.7 0.7 copy-start.4
  94.6 7.4 %collective-permute-start.9 = (bf16[512,256]{1,0:T(8,128)(2,1)S(1)}, bf16[512,256]{1,0:T(8,128)(2,1)S(1)}, u32[]{:S(2)}, u32[]{:S(2)}) collective-permute-start(bf16[512,256]{1,0:T(8,128)(2,1)S(1)} %add_convert_fusion), channel_id=1, source_target_pairs={{0,253},{1,254},{2,255},{3,0},{4,1},{5,2},{6,3},{7,4},{8,5},{9,6},... | collective-permute-start | bytes 786440 | tf_op jit(solution)/shard_map/ppermute | solution.py:17

commit v3 on v2

--- a/solution.py
+++ b/solution.py
@@ -90,7 +90,8 @@
     scale = width ** (-0.5)
     has_in = dq_in is not None
     col_spec = pl.BlockSpec((rows, GROUP * width), lambda g, info: (0, g))
-    kv_spec = pl.BlockSpec((rows, 2 * width), lambda g, info: (0, 0))
+    kv_spec = pl.BlockSpec(kv.shape, lambda g, info: (0, 0))
+    out_spec = pl.BlockSpec((rows, 2 * width), lambda g, info: (0, 0))
     row_spec = pl.BlockSpec((heads, rows), lambda g, info: (0, 0))
     in_specs = [col_spec, col_spec, kv_spec, row_spec, row_spec]
     args = [queries, grad_out, kv, lse, delta]
@@ -112,7 +113,7 @@
             num_scalar_prefetch=1,
             grid=(heads // GROUP,),
             in_specs=in_specs,
-            out_specs=[col_spec, kv_spec],
+            out_specs=[col_spec, out_spec],
             scratch_shapes=[pltpu.VMEM((rows, GROUP * width), jnp.float32)],
         ),
         input_output_aliases=aliases,
@@ -131,7 +132,9 @@
     rows, width = key_rows.shape
     heads = queries.shape[1] // width
     own_block = block_pair[0]
+    tag = jnp.broadcast_to(own_block.astype(jnp.bfloat16), (16, 2 * width))
     kv = jnp.concatenate([key_rows, value_rows], axis=1)
+    kv = jnp.concatenate([kv, tag], axis=0)
     delta = jnp.einsum(
         "qhd,qhd->hq",
         grad_out.reshape(rows, heads, width),
@@ -139,17 +142,18 @@
         preferred_element_type=jnp.float32,
     )
 
-    visitors = [(kv, block_pair)]
-    for step in range(1, STEPS):
-        visitors.append(passed_along((kv, block_pair), "ctx", step))
+    visitors = [kv]
+    for _ in range(1, STEPS):
+        visitors.append(passed_along(visitors[-1], "ctx", 1))
 
     zero_info = jnp.zeros((1,), jnp.int32)
     dq, sums = tile_step(OWN_TILES, zero_info, queries, grad_out, kv, log_total, delta,
                          None, jnp.float32)
     for step in range(1, STEPS):
         received = passed_along(sums, "ctx", 1)
-        kv_s, block_s = visitors[step]
-        other = jnp.where(block_s[0] < own_block, 0, 1).astype(jnp.int32).reshape(1)
+        kv_s = visitors[step]
+        block_s = kv_s[rows, 0].astype(jnp.int32)
+        other = jnp.where(block_s < own_block, 0, 1).astype(jnp.int32).reshape(1)
         last = step == STEPS - 1
         dq, part = tile_step(VISIT_TILES, other, queries, grad_out, kv_s, log_total, delta,
                              dq, jnp.bfloat16 if last else jnp.float32)

time: 103 us -> 100 us (0.971)
  the two profiles are of different devices: /device:TPU:1 before, /device:TPU:125 now
where the time goes in v3:
time: 100 us; the launch traced here: 98.1 us
  waiting for transfers between devices  45 us (45%)
  Pallas kernels  26.1 us (26%)
  starting transfers between devices  14.1 us (14%)
  local copies, waits for them, and re-layouts  4.86 us (5%)
  other arithmetic  4.69 us (5%)
  between operations  3.44 us (3%)
    ppermute x7, waiting for transfers between devices, passed_along(): return lax.ppermute(value, axis, pairs)  45 us
    pallas_call x4, Pallas kernels, tile_step(): pl.pallas_call(functools.partial(tile_body, tiles, has_in, GROUP, half, w...  26.1 us
    ppermute x7, starting transfers between devices, passed_along(): return lax.ppermute(value, axis, pairs)  14.1 us
    add x2, other arithmetic, device_steps(): sums = received + part  2.22 us
  transfers between devices with their start and end apart: 7, of which 4 were waited for; matrix products, arithmetic and copies ran while one was open for 2% of the time, Pallas kernels for 19%

profile of v3, /device:TPU:125, one launch (start us, length us, event | category | flops | bytes accessed | tf_op | source)
XLA Modules:
  0.0 98.1 jit_solution(14542773975005676326)
XLA Ops:
  0.6 0.0 copy-start
  1.4 1.5 %copy.20 = bf16[64,8,8,128]{3,2,1,0:T(8,128)(2,1)S(1)} copy(bf16[64,8,8,128]{3,1,2,0:T(8,128)(2,1)} %bitcast.25) | data formatting | bytes 2097152
  2.9 0.0 copy-done
  2.9 0.0 copy-start.2
  2.9 0.0 copy-start.3
  2.9 0.3 copy.21
  3.2 0.6 fusion
  3.8 0.7 copy.18.dl_ref
  4.5 0.0 copy-done.2
  4.5 0.0 copy-done.3
  4.6 0.7 fusion.3.kv_ref
  5.3 0.0 copy-start.1
  5.3 7.3 %shard_map.94 = (f32[512,1024]{1,0:T(8,128)}, f32[512,256]{1,0:T(8,128)}) custom-call(s32[1]{0:T(128)} %constant.2.clone.1.info_ref, bf16[512,1024]{1,0:T(8,128)(2,1)} %q_ref.7, bf16[512,1024]{1,0:T(8,128)(2,1)} %do_ref.7, bf16[528,256]{1,0:T(8,128)(2,1)} %fusion.3.kv_ref, f32[8,512]{1,0:T(8,128)} %lse_ref.7, f32[8,512]{1,0:T(8,128)} %copy.18.dl_ref), custom_call_target="tpu_custom_call" | custom-call | flops 2013265920 | bytes 4456448 | tf_op jit(solution)/shard_map/pallas_call | solution.py:106
  12.6 1.5 %collective-permute-start.3 = (f32[512,256]{1,0:T(8,128)}, f32[512,256]{1,0:T(8,128)S(1)}, u32[]{:S(2)}, u32[]{:S(2)}) collective-permute-start(f32[512,256]{1,0:T(8,128)} %get-tuple-element.15), channel_id=1, source_target_pairs={{0,1},{1,2},{2,3},{3,4},{4,5},{5,6},{6,7},{7,8},{8,9},{9,10},{10,1... | collective-permute-start | bytes 1572872 | tf_op jit(solution)/shard_map/ppermute | solution.py:17
  14.1 0.0 copy-done.1
  14.1 0.1 collective-permute-start
  14.2 9.1 %collective-permute-done.kv_ref = bf16[528,256]{1,0:T(8,128)(2,1)S(1)} collective-permute-done((bf16[528,256]{1,0:T(8,128)(2,1)S(1)}, bf16[528,256]{1,0:T(8,128)(2,1)S(1)}, u32[]{:S(2)}, u32[]{:S(2)}) %collective-permute-start) | collective-permute-done | bytes 270368 | tf_op jit(solution)/shard_map/ppermute | solution.py:17
  23.3 0.0 copy-start.4
  23.3 0.6 slice.22
  24.5 0.0 copy-done.4
  24.5 6.3 %shard_map.95 = (f32[512,1024]{1,0:T(8,128)}, f32[512,256]{1,0:T(8,128)}) custom-call(s32[1]{0:T(128)} %bitcast.8.info_ref, bf16[512,1024]{1,0:T(8,128)(2,1)} %q_ref.7, bf16[512,1024]{1,0:T(8,128)(2,1)} %do_ref.7, bf16[528,256]{1,0:T(8,128)(2,1)} %copy-done.4, f32[8,512]{1,0:T(8,128)} %lse_ref.7, ...), custom_call_target="tpu_custom_call", output_to_operand_aliasing={{0}: (6, {})} | custom-call | flops 1342177280 | bytes 6553600 | tf_op jit(solution)/shard_map/pallas_call | solution.py:106
  30.9 0.0 collective-permute-done.3
  30.9 1.1 %add.11 = f32[512,256]{1,0:T(8,128)S(1)} add(f32[512,256]{1,0:T(8,128)S(1)} %collective-permute-done.3, f32[512,256]{1,0:T(8,128)} %get-tuple-element.16) | non-fusion elementwise | flops 131072 | bytes 1572864 | tf_op jit(solution)/shard_map/add | solution.py:160
  32.0 2.6 %collective-permute-start.4 = (f32[512,256]{1,0:T(8,128)S(1)}, f32[512,256]{1,0:T(8,128)S(1)}, u32[]{:S(2)}, u32[]{:S(2)}) collective-permute-start(f32[512,256]{1,0:T(8,128)S(1)} %add.11), channel_id=1, source_target_pairs={{0,1},{1,2},{2,3},{3,4},{4,5},{5,6},{6,7},{7,8},{8,9},{9,10},{10,1... | collective-permute-start | bytes 1572872 | tf_op jit(solution)/shard_map/ppermute | solution.py:17
  34.5 0.3 collective-permute-start.1
  34.9 8.8 %collective-permute-done.1.kv_ref = bf16[528,256]{1,0:T(8,128)(2,1)S(1)} collective-permute-done((bf16[528,256]{1,0:T(8,128)(2,1)}, bf16[528,256]{1,0:T(8,128)(2,1)S(1)}, u32[]{:S(2)}, u32[]{:S(2)}) %collective-permute-start.1) | collective-permute-done | bytes 270368 | tf_op jit(solution)/shard_map/ppermute | solution.py:17
  43.7 0.0 copy-start.5
  43.7 0.5 slice.21
  44.9 0.0 copy-done.5
  44.9 6.3 %shard_map.96 = (f32[512,1024]{1,0:T(8,128)}, f32[512,256]{1,0:T(8,128)}) custom-call(s32[1]{0:T(128)} %bitcast.6.info_ref, bf16[512,1024]{1,0:T(8,128)(2,1)} %q_ref.7, bf16[512,1024]{1,0:T(8,128)(2,1)} %do_ref.7, bf16[528,256]{1,0:T(8,128)(2,1)} %copy-done.5, f32[8,512]{1,0:T(8,128)} %lse_ref.7, ...), custom_call_target="tpu_custom_call", output_to_operand_aliasing={{0}: (6, {})} | custom-call | flops 1342177280 | bytes 6553600 | tf_op jit(solution)/shard_map/pallas_call | solution.py:106
  51.2 0.0 collective-permute-done.4
  51.2 1.1 %add.12 = f32[512,256]{1,0:T(8,128)S(1)} add(f32[512,256]{1,0:T(8,128)S(1)} %collective-permute-done.4, f32[512,256]{1,0:T(8,128)} %get-tuple-element.17) | non-fusion elementwise | flops 131072 | bytes 1572864 | tf_op jit(solution)/shard_map/add | solution.py:160
  52.3 2.5 %collective-permute-start.5 = (f32[512,256]{1,0:T(8,128)S(1)}, f32[512,256]{1,0:T(8,128)S(1)}, u32[]{:S(2)}, u32[]{:S(2)}) collective-permute-start(f32[512,256]{1,0:T(8,128)S(1)} %add.12), channel_id=1, source_target_pairs={{0,1},{1,2},{2,3},{3,4},{4,5},{5,6},{6,7},{7,8},{8,9},{9,10},{10,1... | collective-permute-start | bytes 1572872 | tf_op jit(solution)/shard_map/ppermute | solution.py:17
  54.8 5.9 %collective-permute-start.2 = (bf16[528,256]{1,0:T(8,128)(2,1)}, bf16[528,256]{1,0:T(8,128)(2,1)S(1)}, u32[]{:S(2)}, u32[]{:S(2)}) collective-permute-start(bf16[528,256]{1,0:T(8,128)(2,1)} %copy-done.5), channel_id=1, source_target_pairs={{0,1},{1,2},{2,3},{3,4},{4,5},{5,6},{6,7},{7,8},{8,9},{9,10},{10,1... | collective-permute-start | bytes 811016 | tf_op jit(solution)/shard_map/ppermute | solution.py:17
  60.6 3.7 %collective-permute-done.2.kv_ref = bf16[528,256]{1,0:T(8,128)(2,1)S(1)} collective-permute-done((bf16[528,256]{1,0:T(8,128)(2,1)}, bf16[528,256]{1,0:T(8,128)(2,1)S(1)}, u32[]{:S(2)}, u32[]{:S(2)}) %collective-permute-start.2) | collective-permute-done | bytes 270368 | tf_op jit(solution)/shard_map/ppermute | solution.py:17
  64.4 0.0 copy-start.6
  64.4 0.5 slice.20
  65.6 0.0 copy-done.6
  65.6 6.1 %shard_map.97 = (bf16[512,1024]{1,0:T(8,128)(2,1)}, f32[512,256]{1,0:T(8,128)}) custom-call(s32[1]{0:T(128)} %bitcast.4.info_ref, bf16[512,1024]{1,0:T(8,128)(2,1)} %q_ref.7, bf16[512,1024]{1,0:T(8,128)(2,1)} %do_ref.7, bf16[528,256]{1,0:T(8,128)(2,1)} %copy-done.6, f32[8,512]{1,0:T(8,128)} %lse_ref.7, f32[8,512]{1,0:T(8,128)} %copy.18.dl_ref, ...), custom_call_target="tpu_custom_call" | custom-call | flops 1342177280 | bytes 6553600 | tf_op jit(solution)/shard_map/pallas_call | solution.py:106
  71.7 0.0 collective-permute-done.5
  71.7 1.1 %add_convert_fusion = bf16[512,256]{1,0:T(8,128)(2,1)S(1)} fusion(f32[512,256]{1,0:T(8,128)S(1)} %collective-permute-done.5, f32[512,256]{1,0:T(8,128)} %get-tuple-element.18), kind=kLoop, calls=%fused_computation.5 | loop fusion | flops 262144 | bytes 1310720 | tf_op jit(solution)/shard_map/convert_element_type | solution.py:161
  72.8 1.3 %collective-permute-start.6 = (bf16[512,256]{1,0:T(8,128)(2,1)S(1)}, bf16[512,256]{1,0:T(8,128)(2,1)S(1)}, u32[]{:S(2)}, u32[]{:S(2)}) collective-permute-start(bf16[512,256]{1,0:T(8,128)(2,1)S(1)} %add_convert_fusion), channel_id=1, source_target_pairs={{0,253},{1,254},{2,255},{3,0},{4,1},{5,2},{6,3},{7,4},{8,5},{9,6},... | collective-permute-start | bytes 786440 | tf_op jit(solution)/shard_map/ppermute | solution.py:17
  74.1 23.3 %collective-permute-done.6 = bf16[512,256]{1,0:T(8,128)(2,1)S(1)} collective-permute-done((bf16[512,256]{1,0:T(8,128)(2,1)S(1)}, bf16[512,256]{1,0:T(8,128)(2,1)S(1)}, u32[]{:S(2)}, u32[]{:S(2)}) %collective-permute-start.6) | collective-permute-done | bytes 262176 | tf_op jit(solution)/shard_map/ppermute | solution.py:17
  97.4 0.7 fusion.4
Async XLA Ops:
  0.6 2.3 %copy-start = (bf16[512,1024]{1,0:T(8,128)(2,1)S(1)}, bf16[512,1024]{1,0:T(8,128)(2,1)}, u32[]{:S(2)}) copy-start(bf16[512,1024]{1,0:T(8,128)(2,1)} %param.11) | copy-start | bytes 3145732
  2.9 1.7 %copy-start.2 = (bf16[512,128]{1,0:T(8,128)(2,1)S(1)}, bf16[512,128]{1,0:T(8,128)(2,1)}, u32[]{:S(2)}) copy-start(bf16[512,128]{1,0:T(8,128)(2,1)} %param.9) | copy-start | bytes 393220
  2.9 1.6 %copy-start.3 = (bf16[512,128]{1,0:T(8,128)(2,1)S(1)}, bf16[512,128]{1,0:T(8,128)(2,1)}, u32[]{:S(2)}) copy-start(bf16[512,128]{1,0:T(8,128)(2,1)} %param.8) | copy-start | bytes 393220
  5.3 8.8 %copy-start.1 = (bf16[528,256]{1,0:T(8,128)(2,1)S(1)}, bf16[528,256]{1,0:T(8,128)(2,1)}, u32[]{:S(2)}) copy-start(bf16[528,256]{1,0:T(8,128)(2,1)} %fusion.3.kv_ref) | copy-start | bytes 811012
  12.6 18.3 %collective-permute-start.3 = (f32[512,256]{1,0:T(8,128)}, f32[512,256]{1,0:T(8,128)S(1)}, u32[]{:S(2)}, u32[]{:S(2)}) collective-permute-start(f32[512,256]{1,0:T(8,128)} %get-tuple-element.15), channel_id=1, source_target_pairs={{0,1},{1,2},{2,3},{3,4},{4,5},{5,6},{6,7},{7,8},{8,9},{9,10},{10,1... | collective-permute-start | bytes 1572872 | tf_op jit(solution)/shard_map/ppermute | solution.py:17
  14.1 9.2 %collective-permute-start = (bf16[528,256]{1,0:T(8,128)(2,1)S(1)}, bf16[528,256]{1,0:T(8,128)(2,1)S(1)}, u32[]{:S(2)}, u32[]{:S(2)}) collective-permute-start(bf16[528,256]{1,0:T(8,128)(2,1)S(1)} %copy-done.1), channel_id=1, source_target_pairs={{0,1},{1,2},{2,3},{3,4},{4,5},{5,6},{6,7},{7,8},{8,9},{9,10},{10,1... | collective-permute-start | bytes 811016 | tf_op jit(solution)/shard_map/ppermute | solution.py:17
  23.3 1.2 %copy-start.4 = (bf16[528,256]{1,0:T(8,128)(2,1)}, bf16[528,256]{1,0:T(8,128)(2,1)S(1)}, u32[]{:S(2)}) copy-start(bf16[528,256]{1,0:T(8,128)(2,1)S(1)} %collective-permute-done.kv_ref) | copy-start | bytes 811012
  32.0 19.2 %collective-permute-start.4 = (f32[512,256]{1,0:T(8,128)S(1)}, f32[512,256]{1,0:T(8,128)S(1)}, u32[]{:S(2)}, u32[]{:S(2)}) collective-permute-start(f32[512,256]{1,0:T(8,128)S(1)} %add.11), channel_id=1, source_target_pairs={{0,1},{1,2},{2,3},{3,4},{4,5},{5,6},{6,7},{7,8},{8,9},{9,10},{10,1... | collective-permute-start | bytes 1572872 | tf_op jit(solution)/shard_map/ppermute | solution.py:17
  34.5 9.1 %collective-permute-start.1 = (bf16[528,256]{1,0:T(8,128)(2,1)}, bf16[528,256]{1,0:T(8,128)(2,1)S(1)}, u32[]{:S(2)}, u32[]{:S(2)}) collective-permute-start(bf16[528,256]{1,0:T(8,128)(2,1)} %copy-done.4), channel_id=1, source_target_pairs={{0,1},{1,2},{2,3},{3,4},{4,5},{5,6},{6,7},{7,8},{8,9},{9,10},{10,1... | collective-permute-start | bytes 811016 | tf_op jit(solution)/shard_map/ppermute | solution.py:17
  43.7 1.2 %copy-start.5 = (bf16[528,256]{1,0:T(8,128)(2,1)}, bf16[528,256]{1,0:T(8,128)(2,1)S(1)}, u32[]{:S(2)}) copy-start(bf16[528,256]{1,0:T(8,128)(2,1)S(1)} %collective-permute-done.1.kv_ref) | copy-start | bytes 811012
  52.3 19.4 %collective-permute-start.5 = (f32[512,256]{1,0:T(8,128)S(1)}, f32[512,256]{1,0:T(8,128)S(1)}, u32[]{:S(2)}, u32[]{:S(2)}) collective-permute-start(f32[512,256]{1,0:T(8,128)S(1)} %add.12), channel_id=1, source_target_pairs={{0,1},{1,2},{2,3},{3,4},{4,5},{5,6},{6,7},{7,8},{8,9},{9,10},{10,1... | collective-permute-start | bytes 1572872 | tf_op jit(solution)/shard_map/ppermute | solution.py:17
  54.8 9.6 %collective-permute-start.2 = (bf16[528,256]{1,0:T(8,128)(2,1)}, bf16[528,256]{1,0:T(8,128)(2,1)S(1)}, u32[]{:S(2)}, u32[]{:S(2)}) collective-permute-start(bf16[528,256]{1,0:T(8,128)(2,1)} %copy-done.5), channel_id=1, source_target_pairs={{0,1},{1,2},{2,3},{3,4},{4,5},{5,6},{6,7},{7,8},{8,9},{9,10},{10,1... | collective-permute-start | bytes 811016 | tf_op jit(solution)/shard_map/ppermute | solution.py:17
  64.4 1.2 %copy-start.6 = (bf16[528,256]{1,0:T(8,128)(2,1)}, bf16[528,256]{1,0:T(8,128)(2,1)S(1)}, u32[]{:S(2)}) copy-start(bf16[528,256]{1,0:T(8,128)(2,1)S(1)} %collective-permute-done.2.kv_ref) | copy-start | bytes 811012
  72.8 24.6 %collective-permute-start.6 = (bf16[512,256]{1,0:T(8,128)(2,1)S(1)}, bf16[512,256]{1,0:T(8,128)(2,1)S(1)}, u32[]{:S(2)}, u32[]{:S(2)}) collective-permute-start(bf16[512,256]{1,0:T(8,128)(2,1)S(1)} %add_convert_fusion), channel_id=1, source_target_pairs={{0,253},{1,254},{2,255},{3,0},{4,1},{5,2},{6,3},{7,4},{8,5},{9,6},... | collective-permute-start | bytes 786440 | tf_op jit(solution)/shard_map/ppermute | solution.py:17
